TPU v7x, 32 devices: a whole 2x2x4 slice. The times are simulated.
32 devices in a mesh: dp: 8 (over y, x, core), tensor: 4 (over z).
Axes of the slice: x: 2, y: 2, z: 4, core: 2. Of those that a mesh axis runs over, the one named last changes fastest.
Arguments:
- inputs: bfloat16 [16384, 768], P(('dp', 'tensor')), may hold values from -6 to 6
- prefix: int32 [16], P('dp'), may hold values from 102 to 512, as said below
- cotangent: bfloat16 [16384, 768], P(('dp', 'tensor')), may hold values from -6 to 6
- w_query: bfloat16 [768, 768], P('dp', 'tensor'), may hold values from -0.3125 to 0.3125
- w_key: bfloat16 [768, 768], P('dp', 'tensor'), may hold values from -0.3125 to 0.3125
- w_value: bfloat16 [768, 768], P('dp', 'tensor'), may hold values from -0.21875 to 0.21875
- w_out: bfloat16 [768, 768], P('tensor', 'dp'), may hold values from -0.875 to 0.875
- w_up: bfloat16 [768, 3072], P('dp', 'tensor'), may hold values from -0.21875 to 0.21875
- w_down: bfloat16 [3072, 768], P('tensor', 'dp'), may hold values from -0.109375 to 0.109375
- b_query: bfloat16 [768], replicated, may hold values from -3 to 3
- b_value: bfloat16 [768], replicated, may hold values from -3 to 3
- b_out: bfloat16 [768], replicated, may hold values from -2 to 2
- b_up: bfloat16 [3072], replicated, may hold values from -3 to 3
- b_down: bfloat16 [768], replicated, may hold values from -2 to 2
- gain_one: bfloat16 [768], replicated, may hold values from 0.25 to 1.75
- shift_one: bfloat16 [768], replicated, may hold values from -2 to 2
- gain_two: bfloat16 [768], replicated, may hold values from 0.25 to 1.75
- shift_two: bfloat16 [768], replicated, may hold values from -2 to 2
Outputs:
- output: bfloat16 [16384, 768], P(('dp', 'tensor'))
- grad_input: float32 [16384, 768], P(('dp', 'tensor'))
- grad_w_query: float32 [768, 768], P('dp', 'tensor')
- grad_w_key: float32 [768, 768], P('dp', 'tensor')
- grad_w_value: float32 [768, 768], P('dp', 'tensor')
- grad_w_out: float32 [768, 768], P('tensor', 'dp')
- grad_w_up: float32 [768, 3072], P('dp', 'tensor')
- grad_w_down: float32 [3072, 768], P('tensor', 'dp')
- grad_b_query: float32 [768], replicated
- grad_b_value: float32 [768], replicated
- grad_b_out: float32 [768], replicated
- grad_b_up: float32 [3072], replicated
- grad_b_down: float32 [768], replicated
- grad_gain_one: float32 [768], replicated
- grad_shift_one: float32 [768], replicated
- grad_gain_two: float32 [768], replicated
- grad_shift_two: float32 [768], replicated
Inputs may be any that keep to these rules, and one draw needn't show every extreme that they name: Every draw has a sequence whose prefix is exactly 512.
All inputs are finite; a program needn't handle non-finite values.
Results may differ from a plain program's by a relative error of at most 0.015.
Values may be sent and summed in bfloat16 or wider, within the bound.
No kernel may reach another device: no remote copies, remote signals or barrier semaphores. Data moves between devices by JAX's collectives and lax.ppermute only.
A program may use at most 192 MiB of HBM per device.

v0:
```python
import jax
import jax.numpy as jnp
from jax import lax
from jax.sharding import PartitionSpec as P

HEAD = 64
SEQ_LEN = 1024
norm_eps = 1e-12
masked_score = -1e30


def layer_norm(values, norm_gain, norm_shift):
    center = values - jnp.mean(values, axis=-1, keepdims=True)
    spread = jnp.mean(center * center, axis=-1, keepdims=True)
    return center * lax.rsqrt(spread + norm_eps) * norm_gain + norm_shift


def gelu_exact(values):
    return jax.nn.gelu(values, approximate=False)


def dot_right(first_op, second_op):
    return jnp.dot(first_op, second_op, preferred_element_type=jnp.float32)


def dot_back(first_op, second_op):
    return lax.dot_general(
        first_op, second_op, (((1,), (1,)), ((), ())), preferred_element_type=jnp.float32
    )


def dot_over_rows(first_op, second_op):
    return lax.dot_general(
        first_op, second_op, (((0,), (0,)), ((), ())), preferred_element_type=jnp.float32
    )


def block_rows():
    return min(512, SEQ_LEN)


def key_stop(begin_row, block_size):
    prefix_end = -(-(SEQ_LEN // 2) // block_size) * block_size
    return min(SEQ_LEN, max(begin_row + block_size, prefix_end))


def block_scores(queries, key_rows, lengths, begin_row, block_size, stop_key):
    scaling = HEAD ** (-0.5)
    scores = (
        jnp.einsum(
            "sqhe,skhe->shqk",
            queries[:, begin_row : begin_row + block_size],
            key_rows[:, :stop_key],
            preferred_element_type=jnp.float32,
        )
        * scaling
    )
    row_index = begin_row + lax.broadcasted_iota(jnp.int32, (block_size, stop_key), 0)
    col_index = lax.broadcasted_iota(jnp.int32, (block_size, stop_key), 1)
    visible = (col_index <= row_index)[None, None] | (
        col_index[None, None] < lengths[:, None, None, None]
    )
    return jnp.where(visible, scores, masked_score)


def attend_forward(queries, key_rows, value_rows, lengths):
    block_size = block_rows()
    outputs = []
    log_sums = []
    for begin_row in range(0, SEQ_LEN, block_size):
        stop_key = key_stop(begin_row, block_size)
        scores = block_scores(queries, key_rows, lengths, begin_row, block_size, stop_key)
        row_top = jnp.max(scores, axis=-1, keepdims=True)
        exponent = jnp.exp(scores - row_top)
        row_total = jnp.sum(exponent, axis=-1, keepdims=True)
        probability = (exponent / row_total).astype(jnp.bfloat16)
        outputs.append(
            jnp.einsum(
                "shqk,skhe->sqhe",
                probability,
                value_rows[:, :stop_key],
                preferred_element_type=jnp.float32,
            )
        )
        log_sums.append(row_top[..., 0] + jnp.log(row_total[..., 0]))
    return (jnp.concatenate(outputs, axis=1), jnp.concatenate(log_sums, axis=2))


def attend_backward(queries, key_rows, value_rows, grad_attn, log_sums, lengths):
    block_size = block_rows()
    scaling = HEAD ** (-0.5)
    grad_queries = []
    grad_keys = jnp.zeros(key_rows.shape, jnp.float32)
    grad_values = jnp.zeros(value_rows.shape, jnp.float32)
    for begin_row in range(0, SEQ_LEN, block_size):
        stop_key = key_stop(begin_row, block_size)
        scores = block_scores(queries, key_rows, lengths, begin_row, block_size, stop_key)
        probability = jnp.exp(scores - log_sums[:, :, begin_row : begin_row + block_size, None])
        grad_block = grad_attn[:, begin_row : begin_row + block_size]
        grad_prob = jnp.einsum(
            "sqhe,skhe->shqk",
            grad_block,
            value_rows[:, :stop_key],
            preferred_element_type=jnp.float32,
        )
        row_delta = jnp.sum(probability * grad_prob, axis=-1, keepdims=True)
        grad_scores = (probability * (grad_prob - row_delta)).astype(jnp.bfloat16)
        grad_queries.append(
            jnp.einsum(
                "shqk,skhe->sqhe",
                grad_scores,
                key_rows[:, :stop_key],
                preferred_element_type=jnp.float32,
            )
            * scaling
        )
        key_part = (
            jnp.einsum(
                "shqk,sqhe->skhe",
                grad_scores,
                queries[:, begin_row : begin_row + block_size],
                preferred_element_type=jnp.float32,
            )
            * scaling
        )
        grad_keys = grad_keys.at[:, :stop_key].add(key_part)
        value_part = jnp.einsum(
            "shqk,sqhe->skhe",
            probability.astype(jnp.bfloat16),
            grad_block,
            preferred_element_type=jnp.float32,
        )
        grad_values = grad_values.at[:, :stop_key].add(value_part)
    return (jnp.concatenate(grad_queries, axis=1), grad_keys, grad_values)


def placed(segment, total_width, part_index):
    empty = jnp.zeros((total_width,), jnp.float32)
    return lax.dynamic_update_slice_in_dim(empty, segment, part_index * segment.shape[0], 0)


def body(
    inputs,
    prefix,
    cotangent,
    w_query,
    w_key,
    w_value,
    w_out,
    w_up,
    w_down,
    b_query,
    b_value,
    b_out,
    b_up,
    b_down,
    gain_one,
    shift_one,
    gain_two,
    shift_two,
):
    float_type = jnp.float32
    half_type = jnp.bfloat16
    part_index = lax.axis_index("tensor")
    full_query, full_key, full_value, full_out = (
        lax.all_gather(w_query, "dp", axis=0, tiled=True),
        lax.all_gather(w_key, "dp", axis=0, tiled=True),
        lax.all_gather(w_value, "dp", axis=0, tiled=True),
        lax.all_gather(w_out, "dp", axis=1, tiled=True),
    )
    full_up, full_down = (
        lax.all_gather(w_up, "dp", axis=0, tiled=True),
        lax.all_gather(w_down, "dp", axis=1, tiled=True),
    )
    head_width = full_query.shape[1]
    ff_width = full_up.shape[1]
    heads_here = head_width // HEAD
    bias_query = lax.dynamic_slice_in_dim(
        b_query.astype(float_type), part_index * head_width, head_width
    )
    bias_value = lax.dynamic_slice_in_dim(
        b_value.astype(float_type), part_index * head_width, head_width
    )
    bias_up = lax.dynamic_slice_in_dim(b_up.astype(float_type), part_index * ff_width, ff_width)
    gain_first = gain_one.astype(float_type)
    shift_first = shift_one.astype(float_type)
    gain_second = gain_two.astype(float_type)
    shift_second = shift_two.astype(float_type)
    in_rows = inputs.astype(float_type)
    norm_first = layer_norm(in_rows, gain_first, shift_first)
    normed_one = lax.all_gather(norm_first.astype(half_type), "tensor", axis=0, tiled=True)
    seq_count = normed_one.shape[0] // SEQ_LEN
    stacked = jnp.concatenate([full_query, full_key, full_value], axis=1)
    projected = dot_right(normed_one, stacked)
    shape_four = (seq_count, SEQ_LEN, heads_here, HEAD)
    queries = (projected[:, :head_width] + bias_query).astype(half_type).reshape(shape_four)
    key_rows = projected[:, head_width : 2 * head_width].astype(half_type).reshape(shape_four)
    value_rows = (projected[:, 2 * head_width :] + bias_value).astype(half_type).reshape(shape_four)
    attended, log_sums = attend_forward(queries, key_rows, value_rows, prefix)
    attended = attended.reshape(-1, head_width).astype(half_type)
    attn_piece = lax.psum_scatter(
        dot_right(attended, full_out), "tensor", scatter_dimension=0, tiled=True
    )
    middle = in_rows + attn_piece + b_out.astype(float_type)
    norm_second = layer_norm(middle, gain_second, shift_second)
    normed_two = lax.all_gather(norm_second.astype(half_type), "tensor", axis=0, tiled=True)
    pre_act = dot_right(normed_two, full_up) + bias_up
    activated = gelu_exact(pre_act).astype(half_type)
    ff_piece = lax.psum_scatter(
        dot_right(activated, full_down).astype(jnp.bfloat16),
        "tensor",
        scatter_dimension=0,
        tiled=True,
    ).astype(jnp.float32)
    result = (middle + ff_piece + b_down.astype(float_type)).astype(half_type)
    grad_result = cotangent.astype(float_type)
    grad_ff_rows = lax.all_gather(cotangent, "tensor", axis=0, tiled=True)
    grad_act = dot_back(grad_ff_rows, full_down)
    grad_down = dot_over_rows(activated, grad_ff_rows)
    grad_pre = jax.vjp(gelu_exact, pre_act)[1](grad_act)[0].astype(half_type)
    grad_bias_up = jnp.sum(grad_pre, axis=0, dtype=float_type)
    grad_up = dot_over_rows(normed_two, grad_pre)
    grad_norm_two = lax.psum_scatter(
        dot_back(grad_pre, full_up), "tensor", scatter_dimension=0, tiled=True
    )
    norm_two_back = jax.vjp(layer_norm, middle, gain_second, shift_second)[1](grad_norm_two)
    grad_middle = grad_result + norm_two_back[0]
    grad_attn_rows = lax.all_gather(grad_middle.astype(half_type), "tensor", axis=0, tiled=True)
    grad_attended = dot_back(grad_attn_rows, full_out).astype(half_type)
    grad_out_proj = dot_over_rows(attended, grad_attn_rows)
    grad_queries, grad_keys, grad_values = attend_backward(
        queries, key_rows, value_rows, grad_attended.reshape(shape_four), log_sums, prefix
    )
    grads_joined = jnp.concatenate(
        [
            grad_queries.reshape(-1, head_width),
            grad_keys.reshape(-1, head_width),
            grad_values.reshape(-1, head_width),
        ],
        axis=1,
    ).astype(half_type)
    grad_stacked = dot_over_rows(normed_one, grads_joined)
    column_sums = jnp.sum(grads_joined, axis=0, dtype=float_type)
    grad_norm_one = lax.psum_scatter(
        dot_back(grads_joined, stacked).astype(jnp.bfloat16),
        "tensor",
        scatter_dimension=0,
        tiled=True,
    ).astype(jnp.float32)
    norm_one_back = jax.vjp(layer_norm, in_rows, gain_first, shift_first)[1](grad_norm_one)
    grad_input = grad_middle + norm_one_back[0]
    grad_query = grad_stacked[:, :head_width]
    grad_key = grad_stacked[:, head_width : 2 * head_width]
    grad_value = grad_stacked[:, 2 * head_width :]
    shard_query, shard_key, shard_value, shard_out, shard_up, shard_down = (
        lax.psum_scatter(grad_query, "dp", scatter_dimension=0, tiled=True),
        lax.psum_scatter(grad_key, "dp", scatter_dimension=0, tiled=True),
        lax.psum_scatter(grad_value, "dp", scatter_dimension=0, tiled=True),
        lax.psum_scatter(grad_out_proj, "dp", scatter_dimension=1, tiled=True),
        lax.psum_scatter(grad_up, "dp", scatter_dimension=0, tiled=True),
        lax.psum_scatter(grad_down, "dp", scatter_dimension=1, tiled=True),
    )
    vector_sums = lax.psum(
        (
            placed(column_sums[:head_width], b_query.shape[0], part_index),
            placed(column_sums[2 * head_width :], b_value.shape[0], part_index),
            jnp.sum(grad_middle, axis=0),
            placed(grad_bias_up, b_up.shape[0], part_index),
            jnp.sum(grad_result, axis=0),
            norm_one_back[1],
            norm_one_back[2],
            norm_two_back[1],
            norm_two_back[2],
        ),
        ("dp", "tensor"),
    )
    return (
        result,
        grad_input,
        shard_query,
        shard_key,
        shard_value,
        shard_out,
        shard_up,
        shard_down,
        vector_sums[0],
        vector_sums[1],
        vector_sums[2],
        vector_sums[3],
        vector_sums[4],
        vector_sums[5],
        vector_sums[6],
        vector_sums[7],
        vector_sums[8],
    )


def solution(mesh):
    placed = (
        P(("dp", "tensor"), None),
        P("dp"),
        P(("dp", "tensor"), None),
        P("dp", "tensor"),
        P("dp", "tensor"),
        P("dp", "tensor"),
        P("tensor", "dp"),
        P("dp", "tensor"),
        P("tensor", "dp"),
        P(),
        P(),
        P(),
        P(),
        P(),
        P(),
        P(),
        P(),
        P(),
    )
    return jax.shard_map(
        body,
        mesh=mesh,
        in_specs=placed,
        out_specs=(
            P(("dp", "tensor"), None),
            P(("dp", "tensor"), None),
            P("dp", "tensor"),
            P("dp", "tensor"),
            P("dp", "tensor"),
            P("tensor", "dp"),
            P("dp", "tensor"),
            P("tensor", "dp"),
            P(),
            P(),
            P(),
            P(),
            P(),
            P(),
            P(),
            P(),
            P(),
        ),
        check_vma=False,
    )
```

profile of v0, /device:TPU:0, one launch (start us, length us, event | category | flops | bytes accessed | tf_op | source)
XLA Modules:
  0.0 988.7 jit_solution(17090238682944329113)
XLA Ops:
  8.1 1.3 convert_reduce_fusion.3
  9.5 1.5 fusion.28
  13.0 2.4 fusion.27
  15.7 11.1 %all_gather.34 = bf16[192,768]{0,1:T(8,128)(2,1)S(1)} all-gather(bf16[192,96]{0,1:T(8,128)(2,1)S(1)} %copy.81), channel_id=1, replica_groups=mesh['dp'=8,'tensor'=4] {'dp'}, dimensions={1}, use_global_device_ids=true | all-gather | bytes 331776 | tf_op jit(solution)/shard_map/all_gather | solution.py:169
  26.8 9.5 all_gather.31
  36.3 8.6 all_gather.32
  44.9 9.5 all_gather.33
  56.1 1.5 fusion.14
  57.6 24.0 %all-gather.7.cloned.1.call-done = bf16[2048,768]{1,0:T(8,128)(2,1)} async-done(((bf16[512,768]{1,0:T(8,128)(2,1)}), bf16[2048,768]{1,0:T(8,128)(2,1)}) %all-gather.7.cloned.1.call-update) | async-done | bytes 3145744 | tf_op jit(solution)/shard_map/all_gather | solution.py:191
  81.7 4.1 fusion.65
  85.8 2.1 copy-done.13
  88.6 2.4 fusion.33
  94.9 4.2 fusion.83
  99.2 2.8 fusion
  102.0 1.7 copy-done
  103.9 3.3 fusion.48
  107.3 1.4 fusion.84
  109.6 1.7 copy-done.1
  113.6 3.7 fusion.85
  118.7 108.3 %reduce-scatter.19.cloned.1.call-done = f32[512,768]{1,0:T(8,128)} async-done(((f32[2048,768]{1,0:T(8,128)}), f32[512,768]{1,0:T(8,128)}) %reduce-scatter.19.cloned.1.call-update) | async-done | bytes 1572880 | tf_op jit(solution)/shard_map/reduce_scatter | solution.py:201
  227.0 1.7 fusion.78
  232.0 1.4 dynamic-slice_convert_fusion
  233.4 60.8 %all-gather.9.cloned.1.call-done = bf16[2048,768]{1,0:T(8,128)(2,1)} async-done(((bf16[512,768]{1,0:T(8,128)(2,1)}), bf16[2048,768]{1,0:T(8,128)(2,1)}) %all-gather.9.cloned.1.call-update) | async-done | bytes 3145744 | tf_op jit(solution)/shard_map/all_gather | solution.py:206
  294.2 7.5 fusion.86
  301.7 16.7 %all-gather.13.cloned.1.call-done = bf16[768,768]{0,1:T(8,128)(2,1)} async-done(((bf16[768,96]{0,1:T(8,128)(2,1)}), bf16[768,768]{0,1:T(8,128)(2,1)}) %all-gather.13.cloned.1.call-update) | async-done | bytes 1179664 | tf_op jit(solution)/shard_map/all_gather | solution.py:173
  318.4 64.9 %all-gather.15.cloned.1.call-done = bf16[2048,768]{1,0:T(8,128)(2,1)} async-done(((bf16[512,768]{1,0:T(8,128)(2,1)}), bf16[2048,768]{1,0:T(8,128)(2,1)}) %all-gather.15.cloned.1.call-update) | async-done | bytes 3145744 | tf_op jit(solution)/shard_map/all_gather | solution.py:217
  383.3 20.6 %convert_reduce_fusion = (f32[768]{0:T(1024)}, bf16[2048,768]{1,0:T(8,128)(2,1)S(1)}, f32[2048,768]{1,0:T(8,128)}) fusion(f32[2048,768]{1,0:T(8,128)} %fusion.86, f32[768]{0:T(1024)} %dynamic-slice_convert_fusion, bf16[2048,768]{1,0:T(8,128)(2,1)} %all-gather.15.cloned.1.call-done, bf16[768,768]{0,1:T(8,128)(2,1)} %all-gather.13.cloned.1.call-done), kind=kOutput, calls=%fused_computation.11 | convolution fusion | flops 2533883136 | bytes 20060160 | tf_op jit(solution)/shard_map/dot_general | solution.py:27
  403.9 1.7 copy-done.67
  405.6 4.6 fusion.87
  410.3 5.7 multiply_convert_fusion.2
  416.0 1.6 copy-done.15
  417.6 4.0 convolution_convert_fusion.1
  421.7 1.3 convert_element_type.121
  423.0 96.7 %reduce-scatter.23.cloned.1.call-done = f32[512,768]{1,0:T(8,128)} async-done(((f32[2048,768]{1,0:T(8,128)}), f32[512,768]{1,0:T(8,128)}) %reduce-scatter.23.cloned.1.call-update) | async-done | bytes 1572880 | tf_op jit(solution)/shard_map/reduce_scatter | solution.py:223
  519.7 2.6 multiply_reduce_fusion.2
  522.9 60.1 %reduce-scatter.21.cloned.1.call-done = bf16[512,768]{1,0:T(8,128)(2,1)} async-done(((bf16[2048,768]{1,0:T(8,128)(2,1)}), bf16[512,768]{1,0:T(8,128)(2,1)}) %reduce-scatter.21.cloned.1.call-update) | async-done | bytes 786448 | tf_op jit(solution)/shard_map/reduce_scatter | solution.py:209
  583.0 3.3 fusion.77
  588.9 63.1 %all-gather.17.cloned.1.call-done = bf16[2048,768]{1,0:T(8,128)(2,1)} async-done(((bf16[512,768]{1,0:T(8,128)(2,1)}), bf16[2048,768]{1,0:T(8,128)(2,1)}) %all-gather.17.cloned.1.call-update) | async-done | bytes 3145744 | tf_op jit(solution)/shard_map/all_gather | solution.py:228
  652.1 4.0 convolution_convert_fusion.2
  656.0 2.6 reshape.337
  659.2 4.0 fusion.38
  663.2 4.4 multiply_reduce_fusion.1
  667.7 2.6 multiply_convert_fusion.1
  670.3 1.4 fusion.46
  673.9 2.3 convolution_bitcast_fusion
  676.5 10.6 %multiply_reduce_fusion = (f32[2,3,512]{2,1,0:T(4,128)S(1)}, f32[2,3,512,1024]{3,2,1,0:T(8,128)}) fusion(f32[2,3,512,1024]{3,2,1,0:T(8,128)} %copy-done, f32[2,3,512]{2,1,0:T(4,128)S(1)} %log_add_fusion, bf16[2,1024,3,64]{1,0,3,2:T(2,128)(2,1)S(1)} %reshape.334, bf16[2,512,3,64]{1,0,3,2:T(2,128)(2,1)S(1)} %get-tuple-element.165), kind=kOutput, calls=%fused_computation.1 | convolution fusion | flops 412087296 | bytes 26370048 | tf_op jit(solution)/shard_map/sqhe,skhe->shqk/dot_general | solution.py:100
  687.1 6.0 fusion.34
  694.2 6.4 multiply_convert_fusion
  700.6 2.0 fusion.47
  707.1 4.5 convolution_convert_fusion
  711.9 6.9 fusion.89
  718.9 6.9 fusion.88
  725.9 3.9 fusion.90
  733.9 2.2 convert_reduce_fusion.1
  736.4 1.6 copy.106
  738.1 34.4 %reduce-scatter.25.cloned.1.call-done = bf16[512,768]{1,0:T(8,128)(2,1)} async-done(((bf16[2048,768]{1,0:T(8,128)(2,1)}), bf16[512,768]{1,0:T(8,128)(2,1)}) %reduce-scatter.25.cloned.1.call-update) | async-done | bytes 786448 | tf_op jit(solution)/shard_map/reduce_scatter | solution.py:244
  772.5 1.8 convert_reduce_fusion.2
  774.3 2.1 fusion.31
  776.4 2.0 convert_reduce_fusion.4
  778.4 41.5 %all-reduce.2 = (f32[768]{0:T(1024)}, f32[768]{0:T(1024)}, f32[768]{0:T(1024)}, f32[3072]{0:T(1024)}, f32[768]{0:T(1024)}, /*index=5*/f32[768]{0:T(1024)}, f32[768]{0:T(1024)}, f32[768]{0:T(1024)}, f32[768]{0:T(1024)}) all-reduce(f32[768]{0:T(1024)S(1)} %slice_dynamic-update-slice_fusion.1, ...), channel_id=1, replica_groups=mesh['dp'=8,'tensor'=4] {'dp','tensor'}, use_global_device_ids=true, to_apply=%region_25.26 | all-reduce | flops 9216 | bytes 73728 | tf_op jit(solution)/shard_map/psum | solution.py:263
  819.9 45.2 %reduce-scatter.27.cloned.1.call-done = f32[96,768]{1,0:T(8,128)} async-done(((f32[768,768]{1,0:T(8,128)}), f32[96,768]{1,0:T(8,128)}) %reduce-scatter.27.cloned.1.call-update) | async-done | bytes 294928 | tf_op jit(solution)/shard_map/reduce_scatter | solution.py:260
  865.2 38.5 %reduce-scatter.35.cloned.1.call-done = f32[96,192]{1,0:T(8,128)} async-done(((f32[768,192]{1,0:T(8,128)}), f32[96,192]{1,0:T(8,128)}) %reduce-scatter.35.cloned.1.call-update) | async-done | bytes 73744
  903.7 38.7 %reduce-scatter.33.cloned.1.call-done = f32[96,192]{1,0:T(8,128)} async-done(((f32[768,192]{1,0:T(8,128)}), f32[96,192]{1,0:T(8,128)}) %reduce-scatter.33.cloned.1.call-update) | async-done | bytes 73744
  942.4 38.5 %reduce-scatter.31.cloned.1.call-done = f32[96,192]{1,0:T(8,128)} async-done(((f32[768,192]{1,0:T(8,128)}), f32[96,192]{1,0:T(8,128)}) %reduce-scatter.31.cloned.1.call-update) | async-done | bytes 73744
  (238 shorter events, 33.0 us)
Async XLA Ops:
  8.0 7.4 copy-start.63
  8.0 7.5 copy-start.64
  8.0 7.5 copy-start.48
  8.1 18.7 %copy-start.45 = (bf16[96,192]{1,0:T(8,128)(2,1)S(1)}, bf16[96,192]{1,0:T(8,128)(2,1)}, u32[]{:S(2)}) copy-start(bf16[96,192]{1,0:T(8,128)(2,1)} %param.33) | copy-start | bytes 110596
  8.1 28.2 %copy-start.46 = (bf16[96,192]{1,0:T(8,128)(2,1)S(1)}, bf16[96,192]{1,0:T(8,128)(2,1)}, u32[]{:S(2)}) copy-start(bf16[96,192]{1,0:T(8,128)(2,1)} %param.34) | copy-start | bytes 110596
  8.1 36.8 %copy-start.47 = (bf16[96,192]{1,0:T(8,128)(2,1)S(1)}, bf16[96,192]{1,0:T(8,128)(2,1)}, u32[]{:S(2)}) copy-start(bf16[96,192]{1,0:T(8,128)(2,1)} %param.35) | copy-start | bytes 110596
  8.1 46.8 %copy-start.62 = (s32[2]{0:T(128)S(1)}, s32[2]{0:T(128)}, u32[]{:S(2)}) copy-start(s32[2]{0:T(128)} %param.31) | copy-start | bytes 28
  8.1 73.6 %all-gather.7.cloned.1.call-start = ((), (), s32[]{:S(2)}) async-start(), calls=%async_computation.10 | async-start | bytes 3932160 | tf_op jit(solution)/shard_map/all_gather | solution.py:191
  9.5 6.0 copy-start.35
  11.6 3.9 copy-start.49
  12.3 3.2 copy-start.33
  15.3 211.6 %reduce-scatter.19.cloned.1.call-start = ((), (), s32[]{:S(2)}) async-start(), calls=%async_computation.11 | async-start | bytes 7864320 | tf_op jit(solution)/shard_map/reduce_scatter | solution.py:201
  36.3 45.4 %copy-start.26 = (bf16[768,192]{1,0:T(8,128)(2,1)}, bf16[768,192]{1,0:T(8,128)(2,1)S(1)}, u32[]{:S(2)}) copy-start(bf16[768,192]{1,0:T(8,128)(2,1)S(1)} %all_gather.31) | copy-start | bytes 884740
  44.9 36.8 %copy-start.28 = (bf16[768,192]{1,0:T(8,128)(2,1)}, bf16[768,192]{1,0:T(8,128)(2,1)S(1)}, u32[]{:S(2)}) copy-start(bf16[768,192]{1,0:T(8,128)(2,1)S(1)} %all_gather.32) | copy-start | bytes 884740
  54.4 31.3 %copy-start.30 = (bf16[768,192]{1,0:T(8,128)(2,1)}, bf16[768,192]{1,0:T(8,128)(2,1)S(1)}, u32[]{:S(2)}) copy-start(bf16[768,192]{1,0:T(8,128)(2,1)S(1)} %all_gather.33) | copy-start | bytes 884740
  88.6 6.3 copy-start.5
  94.9 4.3 copy-start.16
  94.9 12.3 %copy-start.22 = (bf16[2,512,3,64]{1,0,3,2:T(2,128)(2,1)}, bf16[2,512,3,64]{1,0,3,2:T(2,128)(2,1)S(1)}, u32[]{:S(2)}) copy-start(bf16[2,512,3,64]{1,0,3,2:T(2,128)(2,1)S(1)} %get-tuple-element.166) | copy-start | bytes 1179652
  99.2 4.5 copy-start
  99.2 4.7 copy-start.37
  103.9 3.3 copy-start.39
  103.9 3.3 copy-start.20
  103.9 3.3 copy-start.25
  108.7 2.7 copy-start.41
  108.7 2.7 copy-start.18
  113.6 3.7 copy-start.10
  117.4 109.6 %copy-start.2 = (bf16[512,768]{1,0:T(8,128)(2,1)S(1)}, bf16[512,768]{1,0:T(8,128)(2,1)}, u32[]{:S(2)}) copy-start(bf16[512,768]{1,0:T(8,128)(2,1)} %param.30) | copy-start | bytes 2359300
  117.4 116.0 %all-gather.11.cloned.1.call-start = ((), (), s32[]{:S(2)}) async-start(), calls=%async_computation.13 | async-start | bytes 1327104 | tf_op jit(solution)/shard_map/all_gather | solution.py:172
  118.0 176.2 %all-gather.9.cloned.1.call-start = ((), (), s32[]{:S(2)}) async-start(), calls=%async_computation.12 | async-start | bytes 3932160 | tf_op jit(solution)/shard_map/all_gather | solution.py:206
  230.2 88.1 %all-gather.13.cloned.1.call-start = ((), (), s32[]{:S(2)}) async-start(), calls=%async_computation.14 | async-start | bytes 1327104 | tf_op jit(solution)/shard_map/all_gather | solution.py:173
  230.8 152.5 %all-gather.15.cloned.1.call-start = ((), (), s32[]{:S(2)}) async-start(), calls=%async_computation.16 | async-start | bytes 3932160 | tf_op jit(solution)/shard_map/all_gather | solution.py:217
  231.6 288.1 %reduce-scatter.23.cloned.1.call-start = ((), (), s32[]{:S(2)}) async-start(), calls=%async_computation.17 | async-start | bytes 7864320 | tf_op jit(solution)/shard_map/reduce_scatter | solution.py:223
  383.3 22.3 %copy-start.65 = (bf16[768,768]{1,0:T(8,128)(2,1)S(1)}, bf16[768,768]{1,0:T(8,128)(2,1)}, u32[]{:S(2)}) copy-start(bf16[768,768]{1,0:T(8,128)(2,1)} %all-gather.11.cloned.1.call-done) | copy-start | bytes 3538948
  410.2 172.7 %reduce-scatter.21.cloned.1.call-start = ((), (), s32[]{:S(2)}) async-start(), calls=%async_computation.15 | async-start | bytes 3932160 | tf_op jit(solution)/shard_map/reduce_scatter | solution.py:209
  410.3 7.3 copy-start.66
  421.6 230.4 %all-gather.17.cloned.1.call-start = ((), (), s32[]{:S(2)}) async-start(), calls=%async_computation.18 | async-start | bytes 3932160 | tf_op jit(solution)/shard_map/all_gather | solution.py:228
  583.0 4.4 copy-start.8
  586.3 69.7 %copy-start.53 = (f32[512]{0:T(512)}, f32[512]{0:T(512)S(1)}, u32[]{:S(2)}) copy-start(f32[512]{0:T(512)S(1)} %negate_multiply_fusion.2) | copy-start | bytes 6148
  588.6 147.8 %reduce-scatter.37.cloned.1.call-start = ((), (), s32[]{:S(2)}) async-start(), calls=%async_computation.25 | async-start | bytes 884736
  588.9 74.3 %copy-start.32 = (f32[2,3,512]{2,1,0:T(4,128)}, f32[2,3,512]{2,1,0:T(4,128)S(1)}, u32[]{:S(2)}) copy-start(f32[2,3,512]{2,1,0:T(4,128)S(1)} %log_add_fusion.1) | copy-start | bytes 36868
  659.2 4.0 copy-start.19
  659.2 8.5 slice-start.3
  663.2 4.4 slice-start.4
  667.6 2.6 copy-start.21
  676.2 96.3 %reduce-scatter.25.cloned.1.call-start = ((), (), s32[]{:S(2)}) async-start(), calls=%async_computation.19 | async-start | bytes 3932160 | tf_op jit(solution)/shard_map/reduce_scatter | solution.py:244
  676.5 17.7 %slice-start = ((s8[12582912]{0:T(1024)(128)(4,1)}), s8[4194304]{0:T(1024)(128)(4,1)S(1)}, s32[]{:S(2)}) async-start(s8[12582912]{0:T(1024)(128)(4,1)} %bitcast.80), calls=%async_computation.26 | async-start | bytes 8388608
  676.5 17.7 %slice-start.1 = ((s8[12582912]{0:T(1024)(128)(4,1)}), s8[4194304]{0:T(1024)(128)(4,1)S(1)}, s32[]{:S(2)}) async-start(s8[12582912]{0:T(1024)(128)(4,1)} %bitcast.80), calls=%async_computation.27 | async-start | bytes 8388608
  687.1 7.1 slice-start.2
  694.2 6.4 copy-start.6
  707.1 18.8 %copy-start.12 = (bf16[2048,576]{0,1:T(8,128)(2,1)}, bf16[2048,576]{0,1:T(8,128)(2,1)S(1)}, u32[]{:S(2)}) copy-start(bf16[2048,576]{0,1:T(8,128)(2,1)S(1)} %constant_dynamic-update-slice_fusion) | copy-start | bytes 7077892
  711.6 108.3 %reduce-scatter.29.cloned.1.call-start = ((), (), s32[]{:S(2)}) async-start(), calls=%async_computation.21 | async-start | bytes 2654208 | tf_op jit(solution)/shard_map/reduce_scatter | solution.py:261
  718.9 146.3 %reduce-scatter.27.cloned.1.call-start = ((), (), s32[]{:S(2)}) async-start(), calls=%async_computation.20 | async-start | bytes 2654208 | tf_op jit(solution)/shard_map/reduce_scatter | solution.py:260
  725.8 177.8 %reduce-scatter.35.cloned.1.call-start = ((), (), s32[]{:S(2)}) async-start(), calls=%async_computation.24 | async-start | bytes 884736
  729.8 2.6 copy-start.58
  731.1 211.2 %reduce-scatter.33.cloned.1.call-start = ((), (), s32[]{:S(2)}) async-start(), calls=%async_computation.23 | async-start | bytes 884736
  731.2 41.3 %copy-start.34 = (f32[768]{0:T(1024)S(1)}, f32[768]{0:T(1024)}, u32[]{:S(2)}) copy-start(f32[768]{0:T(1024)} %copy-done.33) | copy-start | bytes 9220
  731.2 41.3 %copy-start.36 = (f32[512]{0:T(512)S(1)}, f32[512]{0:T(512)}, u32[]{:S(2)}) copy-start(f32[512]{0:T(512)} %copy-done.35) | copy-start | bytes 6148
  732.4 248.5 %reduce-scatter.31.cloned.1.call-start = ((), (), s32[]{:S(2)}) async-start(), calls=%async_computation.22 | async-start | bytes 884736
  732.7 41.5 %copy-start.52 = (f32[512]{0:T(512)S(1)}, f32[512]{0:T(512)}, u32[]{:S(2)}) copy-start(f32[512]{0:T(512)} %copy-done.51) | copy-start | bytes 6148
  732.7 41.5 %copy-start.50 = (f32[512]{0:T(512)S(1)}, f32[512]{0:T(512)}, u32[]{:S(2)}) copy-start(f32[512]{0:T(512)} %copy-done.49) | copy-start | bytes 6148
  733.9 42.5 %copy-start.4 = (f32[512,768]{1,0:T(8,128)S(1)}, f32[512,768]{1,0:T(8,128)}, u32[]{:S(2)}) copy-start(f32[512,768]{1,0:T(8,128)} %copy-done.3) | copy-start | bytes 4718596
  733.9 42.5 %copy-start.9 = (bf16[512,768]{1,0:T(8,128)(2,1)S(1)}, bf16[512,768]{1,0:T(8,128)(2,1)}, u32[]{:S(2)}) copy-start(bf16[512,768]{1,0:T(8,128)(2,1)} %param.32) | copy-start | bytes 2359300
  733.9 42.5 %copy-start.54 = (f32[512]{0:T(512)S(1)}, f32[512]{0:T(512)}, u32[]{:S(2)}) copy-start(f32[512]{0:T(512)} %copy-done.53) | copy-start | bytes 6148
  772.5 3.9 copy-start.7
  (25 other events, 40.9 us)
Sparse Core Ops, SparseCore 0:
  15.5 66.1 all-gather.6
  117.5 109.4 reduce-scatter.18
  588.7 63.2 all-gather.16
Sparse Core Ops, SparseCore 1:
  119.8 22.4 all-gather.10
  230.3 63.8 all-gather.8
  295.9 22.4 all-gather.12
  320.0 63.3 all-gather.14
  410.3 109.3 reduce-scatter.22
  522.0 60.9 reduce-scatter.20
  676.3 33.5 reduce-scatter.36
  712.0 60.4 reduce-scatter.24
  776.3 42.3 reduce-scatter.28
  822.6 42.5 reduce-scatter.26
  868.8 34.9 reduce-scatter.34
  907.4 34.9 reduce-scatter.32
  945.9 34.9 reduce-scatter.30
where the time goes:
time: 997 us; the launch traced here: 989 us
  waiting for transfers between devices  692 us (69%)
  matrix products  114 us (11%)
  blocking collectives  80.2 us (8%)
  other arithmetic  53 us (5%)
  local copies, waits for them, and re-layouts  30.8 us (3%)
  between operations  17.1 us (2%)
    unnamed x20, waiting for transfers between devices  118 us
    reduce_scatter x1, waiting for transfers between devices, body(): lax.psum_scatter(dot_right(attended, full_out), 'tensor', scatter_dimensi...  108 us
    reduce_scatter x1, waiting for transfers between devices, body(): lax.psum_scatter(dot_back(grad_pre, full_up), 'tensor', scatter_dimension...  96.7 us
    all_gather x1, waiting for transfers between devices, body(): grad_ff_rows = lax.all_gather(cotangent, 'tensor', axis=0, tiled=True)  64.9 us
    all_gather x1, waiting for transfers between devices, body(): lax.all_gather(grad_middle.astype(half_type), 'tensor', axis=0, tiled=True)  63.1 us
    all_gather x1, waiting for transfers between devices, body(): lax.all_gather(norm_second.astype(half_type), 'tensor', axis=0, tiled=True)  60.8 us
    reduce_scatter x1, waiting for transfers between devices, body(): lax.psum_scatter(dot_right(activated, full_down).astype(jnp.bfloat16), 't...  60.1 us
    reduce_scatter x1, waiting for transfers between devices, body(): lax.psum_scatter(grad_up, 'dp', scatter_dimension=0, tiled=True)  45.2 us
  transfers between devices with their start and end apart: 16, of which 13 were waited for; matrix products, arithmetic and copies ran while one was open for 10% of the time, Pallas kernels for 0%

commit v1 on v0

--- a/solution.py
+++ b/solution.py
@@ -214,7 +214,14 @@
     ).astype(jnp.float32)
     result = (middle + ff_piece + b_down.astype(float_type)).astype(half_type)
     grad_result = cotangent.astype(float_type)
-    grad_ff_rows = lax.all_gather(cotangent, "tensor", axis=0, tiled=True)
+    ways = lax.axis_size("tensor")
+    pieces = [cotangent]
+    for far in range(1, ways):
+        pieces.append(
+            lax.ppermute(pieces[far - 1], "tensor", [(d, (d - 1) % ways) for d in range(ways)])
+        )
+    line = jnp.concatenate(pieces, axis=0)
+    grad_ff_rows = jnp.roll(line, lax.axis_index("tensor") * cotangent.shape[0], axis=0)
     grad_act = dot_back(grad_ff_rows, full_down)
     grad_down = dot_over_rows(activated, grad_ff_rows)
     grad_pre = jax.vjp(gelu_exact, pre_act)[1](grad_act)[0].astype(half_type)

time: 997 us -> 967 us (0.970)
  waiting for transfers between devices: 692 us -> 642 us
  local copies, waits for them, and re-layouts: 30.8 us -> 45 us
    ppermute x0 -> x3, waiting for transfers between devices: none -> 95.3 us  [body(): lax.ppermute(pieces[far - 1], 'tensor', [(d, (d - 1) % ways) for d in ran...]
    all_gather x1 -> x0, waiting for transfers between devices: 64.9 us -> none  [body(): grad_ff_rows = lax.all_gather(cotangent, 'tensor', axis=0, tiled=True)]
    all_gather x1, waiting for transfers between devices: 60.8 us -> 0.01 us  [body(): lax.all_gather(norm_second.astype(half_type), 'tensor', axis=0, tiled=True)]
    reduce_scatter x1, waiting for transfers between devices: 45.2 us -> 0.01 us  [body(): lax.psum_scatter(grad_up, 'dp', scatter_dimension=0, tiled=True)]
    reduce_scatter x1, waiting for transfers between devices: 0.01 us -> 44 us  [body(): lax.psum_scatter(grad_down, 'dp', scatter_dimension=1, tiled=True)]
    all_gather x1, waiting for transfers between devices: 16.7 us -> 0.01 us  [body(): lax.all_gather(w_down, 'dp', axis=1, tiled=True)]
    dot_general x4, matrix products: 19.3 us -> 33.7 us  [dot_right(): return jnp.dot(first_op, second_op, preferred_element_type=jnp.float32)]
    unnamed x157 -> x152, local copies, waits for them, and re-layouts: 19 us -> 30.9 us
  transfers between devices with their start and end apart: 16 -> 18, of which waited for: 13 -> 13; matrix products, arithmetic and copies ran while one was open for 10% -> 13% of each run, Pallas kernels for 0% -> 0%
where the time goes in v1:
time: 967 us; the launch traced here: 958 us
  waiting for transfers between devices  642 us (66%)
  matrix products  120 us (12%)
  blocking collectives  80.1 us (8%)
  other arithmetic  49.5 us (5%)
  local copies, waits for them, and re-layouts  45 us (5%)
  between operations  16.8 us (2%)
    unnamed x19, waiting for transfers between devices  117 us
    reduce_scatter x1, waiting for transfers between devices, body(): lax.psum_scatter(dot_right(attended, full_out), 'tensor', scatter_dimensi...  108 us
    reduce_scatter x1, waiting for transfers between devices, body(): lax.psum_scatter(dot_back(grad_pre, full_up), 'tensor', scatter_dimension...  103 us
    ppermute x3, waiting for transfers between devices, body(): lax.ppermute(pieces[far - 1], 'tensor', [(d, (d - 1) % ways) for d in ran...  95.3 us
    all_gather x1, waiting for transfers between devices, body(): lax.all_gather(grad_middle.astype(half_type), 'tensor', axis=0, tiled=True)  61.3 us
    reduce_scatter x1, waiting for transfers between devices, body(): lax.psum_scatter(dot_right(activated, full_down).astype(jnp.bfloat16), 't...  60.1 us
    reduce_scatter x1, waiting for transfers between devices, body(): lax.psum_scatter(grad_down, 'dp', scatter_dimension=1, tiled=True)  44 us
    psum x1, blocking collectives, body(): lax.psum((placed(column_sums[:head_width], b_query.shape[0], part_index),...  41.4 us
  transfers between devices with their start and end apart: 18, of which 13 were waited for; matrix products, arithmetic and copies ran while one was open for 13% of the time, Pallas kernels for 0%

profile of v1, /device:TPU:0, one launch (start us, length us, event | category | flops | bytes accessed | tf_op | source)
XLA Modules:
  0.0 957.7 jit_solution(9549794784340697657)
XLA Ops:
  9.4 1.5 fusion.34
  12.9 2.4 fusion.33
  17.8 11.1 %all_gather.31 = bf16[192,768]{0,1:T(8,128)(2,1)S(1)} all-gather(bf16[192,96]{0,1:T(8,128)(2,1)S(1)} %copy.81), channel_id=1, replica_groups=mesh['dp'=8,'tensor'=4] {'dp'}, dimensions={1}, use_global_device_ids=true | all-gather | bytes 331776 | tf_op jit(solution)/shard_map/all_gather | solution.py:169
  28.8 9.5 all_gather.28
  38.4 8.6 all_gather.29
  47.0 9.5 all_gather.30
  58.2 1.5 fusion.14
  59.7 21.9 %all-gather.6.cloned.1.call-done = bf16[2048,768]{1,0:T(8,128)(2,1)} async-done(((bf16[512,768]{1,0:T(8,128)(2,1)}), bf16[2048,768]{1,0:T(8,128)(2,1)}) %all-gather.6.cloned.1.call-update) | async-done | bytes 3145744 | tf_op jit(solution)/shard_map/all_gather | solution.py:191
  81.6 4.1 fusion.71
  85.7 2.1 copy-done.13
  88.6 2.4 fusion.39
  95.0 4.2 fusion.91
  99.3 2.8 fusion
  102.1 1.6 copy-done
  104.0 3.3 fusion.54
  113.7 3.7 fusion.93
  118.7 108.3 %reduce-scatter.19.cloned.1.call-done = f32[512,768]{1,0:T(8,128)} async-done(((f32[2048,768]{1,0:T(8,128)}), f32[512,768]{1,0:T(8,128)}) %reduce-scatter.19.cloned.1.call-update) | async-done | bytes 1572880 | tf_op jit(solution)/shard_map/reduce_scatter | solution.py:201
  227.0 1.7 fusion.86
  230.3 2.6 collective-permute-start
  233.0 35.0 %collective-permute-done = bf16[512,768]{1,0:T(8,128)(2,1)S(1)} collective-permute-done((bf16[512,768]{1,0:T(8,128)(2,1)S(1)}, bf16[512,768]{1,0:T(8,128)(2,1)S(1)}, u32[]{:S(2)}, u32[]{:S(2)}) %collective-permute-start) | collective-permute-done | bytes 786464 | tf_op jit(solution)/shard_map/ppermute | solution.py:221
  268.9 48.2 %collective-permute-done.1 = bf16[512,768]{1,0:T(8,128)(2,1)} collective-permute-done((bf16[512,768]{1,0:T(8,128)(2,1)S(1)}, bf16[512,768]{1,0:T(8,128)(2,1)}, u32[]{:S(2)}, u32[]{:S(2)}) %collective-permute-start.1) | collective-permute-done | bytes 786464 | tf_op jit(solution)/shard_map/ppermute | solution.py:221
  317.2 1.4 dynamic-slice_convert_fusion
  319.6 2.1 constant_dynamic-update-slice_fusion.6
  321.7 2.1 constant_dynamic-update-slice_fusion.5
  323.7 12.0 %collective-permute-done.2 = bf16[512,768]{1,0:T(8,128)(2,1)} collective-permute-done((bf16[512,768]{1,0:T(8,128)(2,1)}, bf16[512,768]{1,0:T(8,128)(2,1)}, u32[]{:S(2)}, u32[]{:S(2)}) %collective-permute-start.2) | collective-permute-done | bytes 786464 | tf_op jit(solution)/shard_map/ppermute | solution.py:221
  335.8 2.1 constant_dynamic-update-slice_fusion.4
  339.7 2.1 constant_dynamic-update-slice_fusion.1
  341.8 2.1 constant_dynamic-update-slice_fusion
  343.9 19.4 %multiply_convert_fusion.2 = (bf16[2048,768]{1,0:T(8,128)(2,1)}, f32[2048,768]{1,0:T(8,128)}, f32[2048,768]{1,0:T(8,128)}) fusion(f32[768]{0:T(1024)} %dynamic-slice_convert_fusion, bf16[2048,768]{1,0:T(8,128)(2,1)} %all-gather.8.cloned.1.call-done, bf16[768,768]{1,0:T(8,128)(2,1)} %all-gather.10.cloned.1.call-done), kind=kOutput, calls=%fused_computation.17 | convolution fusion | flops 2519728128 | bytes 20057088 | tf_op jit(solution)/shard_map/dot_general | solution.py:23
  363.3 11.1 %convert_reduce_fusion = (f32[768]{0:T(1024)}, bf16[2048,768]{1,0:T(8,128)(2,1)S(1)}) fusion(f32[2048,768]{1,0:T(8,128)} %get-tuple-element.153, bf16[768,768]{0,1:T(8,128)(2,1)} %all-gather.12.cloned.1.call-done, bf16[4096,768]{1,0:T(8,128)(2,1)} %constant_dynamic-update-slice_fusion, s32[]{:T(128)S(6)} %select_n.38, f32[2048,768]{1,0:T(8,128)} %get-tuple-element.171, ...), kind=kOutput, calls=%fused_computation.11 | convolution fusion | flops 2442657024 | bytes 20061188 | tf_op jit(solution)/shard_map/dot_general | solution.py:27
  374.4 1.6 copy-done.61
  376.0 4.5 fusion.94
  380.7 6.6 convolution_convert_fusion.1
  388.8 103.2 %reduce-scatter.23.cloned.1.call-done = f32[512,768]{1,0:T(8,128)} async-done(((f32[2048,768]{1,0:T(8,128)}), f32[512,768]{1,0:T(8,128)}) %reduce-scatter.23.cloned.1.call-update) | async-done | bytes 1572880 | tf_op jit(solution)/shard_map/reduce_scatter | solution.py:230
  492.0 2.6 multiply_reduce_fusion.2
  495.2 60.1 %reduce-scatter.21.cloned.1.call-done = bf16[512,768]{1,0:T(8,128)(2,1)} async-done(((bf16[2048,768]{1,0:T(8,128)(2,1)}), bf16[512,768]{1,0:T(8,128)(2,1)}) %reduce-scatter.21.cloned.1.call-update) | async-done | bytes 786448 | tf_op jit(solution)/shard_map/reduce_scatter | solution.py:209
  555.3 3.2 fusion.84
  563.0 61.3 %all-gather.14.cloned.1.call-done = bf16[2048,768]{1,0:T(8,128)(2,1)} async-done(((bf16[512,768]{1,0:T(8,128)(2,1)}), bf16[2048,768]{1,0:T(8,128)(2,1)}) %all-gather.14.cloned.1.call-update) | async-done | bytes 3145744 | tf_op jit(solution)/shard_map/all_gather | solution.py:235
  624.3 3.1 convolution_convert_fusion.2
  628.5 4.0 fusion.44
  632.6 4.4 multiply_reduce_fusion.1
  637.0 1.8 multiply_convert_fusion.1
  640.3 3.0 fusion.47
  643.2 2.3 convolution_bitcast_fusion
  645.8 10.6 %multiply_reduce_fusion = (f32[2,3,512]{2,1,0:T(4,128)S(1)}, f32[2,3,512,1024]{3,2,1,0:T(8,128)}) fusion(f32[2,3,512,1024]{3,2,1,0:T(8,128)} %copy-done, f32[2,3,512]{2,1,0:T(4,128)S(1)} %log_add_fusion, bf16[2,1024,3,64]{1,0,3,2:T(2,128)(2,1)S(1)} %copy-done.7, bf16[2,512,3,64]{1,0,3,2:T(2,128)(2,1)S(1)} %get-tuple-element.164), kind=kOutput, calls=%fused_computation.1 | convolution fusion | flops 412087296 | bytes 26370048 | tf_op jit(solution)/shard_map/sqhe,skhe->shqk/dot_general | solution.py:100
  656.4 6.0 fusion.40
  663.5 6.4 multiply_convert_fusion
  669.9 2.0 fusion.53
  677.1 4.5 convolution_convert_fusion
  681.9 7.0 fusion.95
  689.0 6.9 fusion.19
  696.0 4.6 fusion.96
  704.3 2.3 copy.99
  706.6 2.1 convert_reduce_fusion.1
  708.9 1.6 copy.106
  710.6 31.2 %reduce-scatter.25.cloned.1.call-done = bf16[512,768]{1,0:T(8,128)(2,1)} async-done(((bf16[2048,768]{1,0:T(8,128)(2,1)}), bf16[512,768]{1,0:T(8,128)(2,1)}) %reduce-scatter.25.cloned.1.call-update) | async-done | bytes 786448 | tf_op jit(solution)/shard_map/reduce_scatter | solution.py:251
  741.8 1.7 convert_reduce_fusion.2
  743.5 2.1 fusion.37
  745.6 3.1 convert_reduce_fusion.4
  748.8 41.4 %all-reduce.2 = (f32[768]{0:T(1024)}, f32[768]{0:T(1024)}, f32[768]{0:T(1024)}, f32[3072]{0:T(1024)}, f32[768]{0:T(1024)}, /*index=5*/f32[768]{0:T(1024)}, f32[768]{0:T(1024)}, f32[768]{0:T(1024)}, f32[768]{0:T(1024)}) all-reduce(f32[768]{0:T(1024)S(1)} %slice_dynamic-update-slice_fusion.1, ...), channel_id=1, replica_groups=mesh['dp'=8,'tensor'=4] {'dp','tensor'}, use_global_device_ids=true, to_apply=%region_25.26 | all-reduce | flops 9216 | bytes 73728 | tf_op jit(solution)/shard_map/psum | solution.py:270
  790.2 44.0 %reduce-scatter.29.cloned.1.call-done = f32[768,96]{0,1:T(8,128)} async-done(((f32[768,768]{0,1:T(8,128)}), f32[768,96]{0,1:T(8,128)}) %reduce-scatter.29.cloned.1.call-update) | async-done | bytes 294928 | tf_op jit(solution)/shard_map/reduce_scatter | solution.py:268
  834.2 38.7 %reduce-scatter.35.cloned.1.call-done = f32[96,192]{1,0:T(8,128)} async-done(((f32[768,192]{1,0:T(8,128)}), f32[96,192]{1,0:T(8,128)}) %reduce-scatter.35.cloned.1.call-update) | async-done | bytes 73744
  872.9 38.6 %reduce-scatter.33.cloned.1.call-done = f32[96,192]{1,0:T(8,128)} async-done(((f32[768,192]{1,0:T(8,128)}), f32[96,192]{1,0:T(8,128)}) %reduce-scatter.33.cloned.1.call-update) | async-done | bytes 73744
  911.4 38.7 %reduce-scatter.31.cloned.1.call-done = f32[96,192]{1,0:T(8,128)} async-done(((f32[768,192]{1,0:T(8,128)}), f32[96,192]{1,0:T(8,128)}) %reduce-scatter.31.cloned.1.call-update) | async-done | bytes 73744
  (236 shorter events, 45.1 us)
Async XLA Ops:
  8.0 20.8 %copy-start.43 = (bf16[96,192]{1,0:T(8,128)(2,1)S(1)}, bf16[96,192]{1,0:T(8,128)(2,1)}, u32[]{:S(2)}) copy-start(bf16[96,192]{1,0:T(8,128)(2,1)} %param.33) | copy-start | bytes 110596
  8.0 30.3 %copy-start.44 = (bf16[96,192]{1,0:T(8,128)(2,1)S(1)}, bf16[96,192]{1,0:T(8,128)(2,1)}, u32[]{:S(2)}) copy-start(bf16[96,192]{1,0:T(8,128)(2,1)} %param.34) | copy-start | bytes 110596
  8.0 38.9 %copy-start.45 = (bf16[96,192]{1,0:T(8,128)(2,1)S(1)}, bf16[96,192]{1,0:T(8,128)(2,1)}, u32[]{:S(2)}) copy-start(bf16[96,192]{1,0:T(8,128)(2,1)} %param.35) | copy-start | bytes 110596
  8.1 48.9 %copy-start.59 = (s32[2]{0:T(128)S(1)}, s32[2]{0:T(128)}, u32[]{:S(2)}) copy-start(s32[2]{0:T(128)} %param.31) | copy-start | bytes 28
  8.1 73.6 %all-gather.6.cloned.1.call-start = ((), (), s32[]{:S(2)}) async-start(), calls=%async_computation.10 | async-start | bytes 3932160 | tf_op jit(solution)/shard_map/all_gather | solution.py:191
  9.4 6.7 copy-start.37
  11.5 4.6 copy-start.46
  12.2 3.9 copy-start.35
  15.3 211.7 %reduce-scatter.19.cloned.1.call-start = ((), (), s32[]{:S(2)}) async-start(), calls=%async_computation.11 | async-start | bytes 7864320 | tf_op jit(solution)/shard_map/reduce_scatter | solution.py:201
  38.4 47.3 %copy-start.27 = (bf16[768,192]{1,0:T(8,128)(2,1)}, bf16[768,192]{1,0:T(8,128)(2,1)S(1)}, u32[]{:S(2)}) copy-start(bf16[768,192]{1,0:T(8,128)(2,1)S(1)} %all_gather.28) | copy-start | bytes 884740
  47.0 38.8 %copy-start.29 = (bf16[768,192]{1,0:T(8,128)(2,1)}, bf16[768,192]{1,0:T(8,128)(2,1)S(1)}, u32[]{:S(2)}) copy-start(bf16[768,192]{1,0:T(8,128)(2,1)S(1)} %all_gather.29) | copy-start | bytes 884740
  56.5 29.2 %copy-start.31 = (bf16[768,192]{1,0:T(8,128)(2,1)}, bf16[768,192]{1,0:T(8,128)(2,1)S(1)}, u32[]{:S(2)}) copy-start(bf16[768,192]{1,0:T(8,128)(2,1)S(1)} %all_gather.30) | copy-start | bytes 884740
  88.6 6.4 copy-start.8
  91.6 10.5 %copy-start.6 = (bf16[2,1024,3,64]{1,0,3,2:T(2,128)(2,1)}, bf16[2,1024,3,64]{1,0,3,2:T(2,128)(2,1)S(1)}, u32[]{:S(2)}) copy-start(bf16[2,1024,3,64]{1,0,3,2:T(2,128)(2,1)S(1)} %reshape.334) | copy-start | bytes 2359300
  95.0 4.3 copy-start.18
  95.0 12.3 %copy-start.24 = (bf16[2,512,3,64]{1,0,3,2:T(2,128)(2,1)}, bf16[2,512,3,64]{1,0,3,2:T(2,128)(2,1)S(1)}, u32[]{:S(2)}) copy-start(bf16[2,512,3,64]{1,0,3,2:T(2,128)(2,1)S(1)} %get-tuple-element.165) | copy-start | bytes 1179652
  99.2 4.5 copy-start
  99.2 4.7 copy-start.39
  104.0 3.3 copy-start.40
  104.0 3.3 copy-start.22
  104.0 3.3 copy-start.26
  108.7 2.9 copy-start.1
  108.7 2.9 copy-start.41
  117.4 109.6 %copy-start.2 = (bf16[512,768]{1,0:T(8,128)(2,1)S(1)}, bf16[512,768]{1,0:T(8,128)(2,1)}, u32[]{:S(2)}) copy-start(bf16[512,768]{1,0:T(8,128)(2,1)} %param.30) | copy-start | bytes 2359300
  117.4 226.5 %all-gather.10.cloned.1.call-start = ((), (), s32[]{:S(2)}) async-start(), calls=%async_computation.13 | async-start | bytes 1327104 | tf_op jit(solution)/shard_map/all_gather | solution.py:172
  118.0 225.9 %all-gather.8.cloned.1.call-start = ((), (), s32[]{:S(2)}) async-start(), calls=%async_computation.12 | async-start | bytes 3932160 | tf_op jit(solution)/shard_map/all_gather | solution.py:206
  118.7 111.6 %copy-start.5 = (bf16[512,768]{1,0:T(8,128)(2,1)S(1)}, bf16[512,768]{1,0:T(8,128)(2,1)}, u32[]{:S(2)}) copy-start(bf16[512,768]{1,0:T(8,128)(2,1)} %param.32) | copy-start | bytes 2359300
  230.3 133.1 %all-gather.12.cloned.1.call-start = ((), (), s32[]{:S(2)}) async-start(), calls=%async_computation.14 | async-start | bytes 1327104 | tf_op jit(solution)/shard_map/all_gather | solution.py:173
  230.3 37.7 %collective-permute-start = (bf16[512,768]{1,0:T(8,128)(2,1)S(1)}, bf16[512,768]{1,0:T(8,128)(2,1)S(1)}, u32[]{:S(2)}, u32[]{:S(2)}) collective-permute-start(bf16[512,768]{1,0:T(8,128)(2,1)S(1)} %copy-done.5), channel_id=1, source_target_pairs={{0,3},{1,0},{2,1},{3,2},{4,7},{5,4},{6,5},{7,6},{8,11},{9,8},{10,9... | collective-permute-start | bytes 2359304 | tf_op jit(solution)/shard_map/ppermute | solution.py:221
  268.9 48.2 %collective-permute-start.1 = (bf16[512,768]{1,0:T(8,128)(2,1)S(1)}, bf16[512,768]{1,0:T(8,128)(2,1)}, u32[]{:S(2)}, u32[]{:S(2)}) collective-permute-start(bf16[512,768]{1,0:T(8,128)(2,1)S(1)} %collective-permute-done), channel_id=1, source_target_pairs={{0,3},{1,0},{2,1},{3,2},{4,7},{5,4},{6,5},{7,6},{8,11},{9,8},{10,9... | collective-permute-start | bytes 2359304 | tf_op jit(solution)/shard_map/ppermute | solution.py:221
  317.1 18.7 %collective-permute-start.2 = (bf16[512,768]{1,0:T(8,128)(2,1)}, bf16[512,768]{1,0:T(8,128)(2,1)}, u32[]{:S(2)}, u32[]{:S(2)}) collective-permute-start(bf16[512,768]{1,0:T(8,128)(2,1)} %collective-permute-done.1), channel_id=1, source_target_pairs={{0,3},{1,0},{2,1},{3,2},{4,7},{5,4},{6,5},{7,6},{8,11},{9,8},{10,9... | collective-permute-start | bytes 2359304 | tf_op jit(solution)/shard_map/ppermute | solution.py:221
  317.1 174.9 %reduce-scatter.23.cloned.1.call-start = ((), (), s32[]{:S(2)}) async-start(), calls=%async_computation.16 | async-start | bytes 7864320 | tf_op jit(solution)/shard_map/reduce_scatter | solution.py:230
  317.2 21.6 %copy-start.15 = (bf16[512,768]{1,0:T(8,128)(2,1)S(1)}, bf16[512,768]{1,0:T(8,128)(2,1)}, u32[]{:S(2)}) copy-start(bf16[512,768]{1,0:T(8,128)(2,1)} %copy-done.14) | copy-start | bytes 2359300
  363.3 12.7 %copy-start.60 = (bf16[768,768]{1,0:T(8,128)(2,1)S(1)}, bf16[768,768]{1,0:T(8,128)(2,1)}, u32[]{:S(2)}) copy-start(bf16[768,768]{1,0:T(8,128)(2,1)} %all-gather.10.cloned.1.call-done) | copy-start | bytes 3538948
  380.6 174.7 %reduce-scatter.21.cloned.1.call-start = ((), (), s32[]{:S(2)}) async-start(), calls=%async_computation.15 | async-start | bytes 3932160 | tf_op jit(solution)/shard_map/reduce_scatter | solution.py:209
  387.3 237.0 %all-gather.14.cloned.1.call-start = ((), (), s32[]{:S(2)}) async-start(), calls=%async_computation.17 | async-start | bytes 3932160 | tf_op jit(solution)/shard_map/all_gather | solution.py:235
  560.8 148.1 %reduce-scatter.37.cloned.1.call-start = ((), (), s32[]{:S(2)}) async-start(), calls=%async_computation.24 | async-start | bytes 884736
  627.9 4.6 copy-start.21
  627.9 4.6 copy-start.33
  628.5 8.5 slice-start.3
  632.5 4.4 slice-start.4
  632.5 4.4 copy-start.34
  638.8 4.4 copy-start.11
  638.9 4.4 copy-start.16
  645.5 96.3 %reduce-scatter.25.cloned.1.call-start = ((), (), s32[]{:S(2)}) async-start(), calls=%async_computation.18 | async-start | bytes 3932160 | tf_op jit(solution)/shard_map/reduce_scatter | solution.py:251
  645.8 17.7 %slice-start = ((s8[12582912]{0:T(1024)(128)(4,1)}), s8[4194304]{0:T(1024)(128)(4,1)S(1)}, s32[]{:S(2)}) async-start(s8[12582912]{0:T(1024)(128)(4,1)} %bitcast.78), calls=%async_computation.25 | async-start | bytes 8388608
  645.8 17.7 %slice-start.1 = ((s8[12582912]{0:T(1024)(128)(4,1)}), s8[4194304]{0:T(1024)(128)(4,1)S(1)}, s32[]{:S(2)}) async-start(s8[12582912]{0:T(1024)(128)(4,1)} %bitcast.78), calls=%async_computation.26 | async-start | bytes 8388608
  656.4 7.1 slice-start.2
  663.5 6.4 copy-start.9
  674.4 2.7 copy-start.28
  681.6 108.5 %reduce-scatter.27.cloned.1.call-start = ((), (), s32[]{:S(2)}) async-start(), calls=%async_computation.19 | async-start | bytes 2654208 | tf_op jit(solution)/shard_map/reduce_scatter | solution.py:267
  688.9 145.3 %reduce-scatter.29.cloned.1.call-start = ((), (), s32[]{:S(2)}) async-start(), calls=%async_computation.20 | async-start | bytes 2654208 | tf_op jit(solution)/shard_map/reduce_scatter | solution.py:268
  695.9 177.0 %reduce-scatter.35.cloned.1.call-start = ((), (), s32[]{:S(2)}) async-start(), calls=%async_computation.23 | async-start | bytes 884736
  700.6 3.4 copy-start.55
  702.6 39.2 %copy-start.36 = (f32[768]{0:T(1024)S(1)}, f32[768]{0:T(1024)}, u32[]{:S(2)}) copy-start(f32[768]{0:T(1024)} %copy-done.35) | copy-start | bytes 9220
  702.6 39.2 %copy-start.38 = (f32[512]{0:T(512)S(1)}, f32[512]{0:T(512)}, u32[]{:S(2)}) copy-start(f32[512]{0:T(512)} %copy-done.37) | copy-start | bytes 6148
  702.7 208.7 %reduce-scatter.33.cloned.1.call-start = ((), (), s32[]{:S(2)}) async-start(), calls=%async_computation.22 | async-start | bytes 884736
  702.7 40.8 %copy-start.49 = (f32[512]{0:T(512)S(1)}, f32[512]{0:T(512)}, u32[]{:S(2)}) copy-start(f32[512]{0:T(512)} %copy-done.48) | copy-start | bytes 6148
  702.7 40.8 %copy-start.47 = (f32[512]{0:T(512)S(1)}, f32[512]{0:T(512)}, u32[]{:S(2)}) copy-start(f32[512]{0:T(512)} %copy-done.46) | copy-start | bytes 6148
  703.9 41.7 %copy-start.4 = (f32[512,768]{1,0:T(8,128)S(1)}, f32[512,768]{1,0:T(8,128)}, u32[]{:S(2)}) copy-start(f32[512,768]{1,0:T(8,128)} %copy-done.3) | copy-start | bytes 4718596
  703.9 41.7 %copy-start.51 = (f32[512]{0:T(512)S(1)}, f32[512]{0:T(512)}, u32[]{:S(2)}) copy-start(f32[512]{0:T(512)} %copy-done.50) | copy-start | bytes 6148
  703.9 246.2 %reduce-scatter.31.cloned.1.call-start = ((), (), s32[]{:S(2)}) async-start(), calls=%async_computation.21 | async-start | bytes 884736
  710.6 38.2 %copy-start.53 = (f32[768]{0:T(1024)S(1)}, f32[768]{0:T(1024)}, u32[]{:S(2)}) copy-start(f32[768]{0:T(1024)} %get-tuple-element.132) | copy-start | bytes 9220
  710.6 38.2 %copy-start.54 = (f32[768]{0:T(1024)S(1)}, f32[768]{0:T(1024)}, u32[]{:S(2)}) copy-start(f32[768]{0:T(1024)} %get-tuple-element.136) | copy-start | bytes 9220
  (21 other events, 32.0 us)
Sparse Core Ops, SparseCore 0:
  15.4 66.1 all-gather.5
  117.5 109.4 reduce-scatter.18
  560.9 63.2 all-gather.13
Sparse Core Ops, SparseCore 1:
  119.8 22.4 all-gather.9
  230.3 87.6 all-gather.7
  319.8 25.8 all-gather.11
  380.7 111.3 reduce-scatter.22
  494.3 60.9 reduce-scatter.20
  645.6 33.5 reduce-scatter.36
  681.7 60.0 reduce-scatter.24
  745.6 42.3 reduce-scatter.26
  791.7 42.4 reduce-scatter.28
  837.9 34.9 reduce-scatter.34
  876.5 34.9 reduce-scatter.32
  915.2 34.9 reduce-scatter.30
